TPU v7x, 512 devices: a whole 4x8x8 slice. The times are simulated.
512 devices in a mesh: atom: 64 (over y, x, z_hi), ka: 8 (over z_lo, core).
Axes of the slice: x: 4, y: 8, z: 8 (z_hi: 2, z_lo: 4; z = z_hi * 4 + z_lo), core: 2. Of those that a mesh axis runs over, the one named last changes fastest.
Arguments:
- features: bfloat16 [131072, 256], P('atom'), may hold values from -6 to 6
- positions: float32 [3, 131072], P(None, 'atom'), may hold values from 0 to 1
- k_indices: int32 [3, 4096], P(None, 'ka'), may hold values from -8 to 8
- species: int32 [131072], P('atom'), may hold values from 0 to 7
- brick_counts: int32 [64], P('atom'), may hold values from 1024 to 2048, as said below
- smearing: float32 [256], replicated, may hold values from 0.01 to 0.03
- teacher_charge: float32 [256], replicated, may hold values from -0.375 to 0.375
- norm_gain: float32 [256], replicated, may hold values from 0.5 to 1.5
- w_mix: bfloat16 [256, 256], replicated, may hold values from -0.375 to 0.375
- w_read: float32 [256], replicated, may hold values from -0.375 to 0.375
- w_student: bfloat16 [256, 128], replicated, may hold values from -0.375 to 0.375
- species_embed: float32 [8, 128], replicated, may hold values from -3 to 3
- w_charge: float32 [128], replicated, may hold values from -0.5 to 0.5
- species_bias: float32 [8], replicated, may hold values from -3 to 3
- student_smear: float32 [1], replicated, may hold values from 0.05 to 0.15
Outputs:
- teacher_features: bfloat16 [131072, 256], P(('atom', 'ka'))
- teacher_forces: float32 [3, 131072], P(None, ('atom', 'ka'))
- student_forces: float32 [3, 131072], P(None, ('atom', 'ka'))
- student_energy: float32 [131072], P(('atom', 'ka'))
- distill_loss: float32 [], replicated
Inputs may be any that keep to these rules, and one draw needn't show every extreme that they name: The first brick_counts[b] atom slots of brick b hold real atoms and the rest are padding; some brick is full in every draw.
All inputs are finite; a program needn't handle non-finite values.
Results may differ from a plain program's by a relative error of at most 0.0075.
Values sent between devices are 32-bit elements; how exact they have to be, the bound alone decides.
No kernel may reach another device: no remote copies, remote signals or barrier semaphores. Data moves between devices by JAX's collectives and lax.ppermute only.
A program may use at most 64 MiB of HBM per device.

v0:
```python
import functools
import math
import jax
import jax.numpy as jnp
from jax import lax
from jax.sharding import Mesh
from jax.sharding import PartitionSpec as P

TWO_PI = 2.0 * math.pi
SCREEN = 20.0
HIGHEST_PRECISION = lax.Precision.HIGHEST
ATOM_AXES = ("y", "x", "zh")
KA_AXES = ("zl", "core")
ALL_AXES = ATOM_AXES + KA_AXES
PAD_ROWS = 256


def phase_table(positions, k_indices):
    k_float = k_indices.astype(jnp.float32)
    products = (
        positions[0][:, None] * k_float[0][None, :]
        + positions[1][:, None] * k_float[1][None, :]
        + positions[2][:, None] * k_float[2][None, :]
    )
    angles = TWO_PI * products
    return jnp.concatenate([jnp.cos(angles), jnp.sin(angles)], axis=1).astype(jnp.bfloat16)


def k_geometry(k_indices):
    k_vectors = TWO_PI * k_indices.astype(jnp.float32)
    k_square = (
        k_vectors[0] * k_vectors[0] + k_vectors[1] * k_vectors[1] + k_vectors[2] * k_vectors[2]
    )
    return (k_vectors, k_square)


def teacher_kernel(k_square, smearing, inv_root):
    spread = (smearing * smearing)[None, :]
    return jnp.exp(-0.5 * k_square[:, None] * spread) / (k_square[:, None] + SCREEN) * inv_root


def student_table(k_vectors, k_square, sums, student_smear, inv_root, k_width):
    spread = student_smear[0] * student_smear[0]
    kernel = jnp.exp(-0.5 * k_square * spread) / (k_square + SCREEN) * inv_root
    cos_part = kernel * sums[:k_width]
    sin_part = kernel * sums[k_width:]
    upper_rows = jnp.stack(
        [
            cos_part,
            -(k_vectors[0] * sin_part),
            -(k_vectors[1] * sin_part),
            -(k_vectors[2] * sin_part),
        ],
        axis=1,
    )
    lower_rows = jnp.stack(
        [sin_part, k_vectors[0] * cos_part, k_vectors[1] * cos_part, k_vectors[2] * cos_part],
        axis=1,
    )
    return jnp.concatenate([upper_rows, lower_rows], axis=0).astype(jnp.bfloat16)


def student_charge(features, species, live_mask, w_student, species_embed, w_charge, species_bias):
    onehot = (
        species[:, None] == jnp.arange(species_embed.shape[0], dtype=jnp.int32)[None, :]
    ).astype(jnp.float32)
    inner_sum = jnp.dot(features, w_student, preferred_element_type=jnp.float32) + jnp.dot(
        onehot, species_embed, precision=HIGHEST_PRECISION
    )
    hidden = jax.nn.silu(inner_sum)
    return (
        jnp.dot(hidden, w_charge, precision=HIGHEST_PRECISION)
        + jnp.dot(onehot, species_bias, precision=HIGHEST_PRECISION)
    ) * live_mask


def finish(
    potential, teacher_force, student_part, features, charge, live_mask, norm_gain, w_mix, w_read
):
    mean_square = jnp.mean(potential * potential, axis=1, keepdims=True)
    normed = (potential * lax.rsqrt(mean_square + 1e-06) * norm_gain[None, :]).astype(jnp.bfloat16)
    update = jax.nn.silu(jnp.dot(normed, w_mix, preferred_element_type=jnp.float32))
    combined = features.astype(jnp.float32) + update
    teacher_energy = jnp.dot(combined, w_read, precision=HIGHEST_PRECISION)
    student_energy = 0.5 * charge * student_part[:, 0]
    forces = charge[:, None] * student_part[:, 1:4]
    misfit = (student_energy - teacher_energy) ** 2 + jnp.sum(
        (forces - teacher_force) ** 2, axis=1
    ) / 3.0
    return (
        combined.astype(jnp.bfloat16),
        teacher_force,
        forces,
        student_energy,
        live_mask * misfit,
    )


def sum_over_atoms(payload):
    part = lax.psum_scatter(payload, "y", scatter_dimension=0, tiled=True)
    part = lax.psum_scatter(part, "x", scatter_dimension=0, tiled=True)
    part = lax.psum(part, "zh")
    part = lax.all_gather(part, "x", axis=0, tiled=True)
    return lax.all_gather(part, "y", axis=0, tiled=True)


def local(
    features,
    positions,
    k_indices,
    species,
    brick_counts,
    smearing,
    teacher_charge,
    norm_gain,
    w_mix,
    w_read,
    w_student,
    species_embed,
    w_charge,
    species_bias,
    student_smear,
):
    atom_rows = features.shape[0]
    k_width = k_indices.shape[1]
    channels = features.shape[1]
    atom_groups = 1
    for axis in ATOM_AXES:
        atom_groups *= lax.axis_size(axis)
    ka_groups = 1
    for axis in KA_AXES:
        ka_groups *= lax.axis_size(axis)
    inv_root = 1.0 / math.sqrt(atom_rows * atom_groups)
    live_mask = (jnp.arange(atom_rows, dtype=jnp.int32) < brick_counts[0]).astype(jnp.float32)
    masked = features * live_mask.astype(jnp.bfloat16)[:, None]
    charge = student_charge(
        features, species, live_mask, w_student, species_embed, w_charge, species_bias
    )
    charge_low = charge.astype(jnp.bfloat16)
    phases = phase_table(positions, k_indices)
    factor = lax.dot_general(
        phases, masked, (((0,), (0,)), ((), ())), preferred_element_type=jnp.float32
    )
    charge_sum = jnp.dot(charge_low, phases, preferred_element_type=jnp.float32)
    extra = jnp.concatenate(
        [
            charge_sum,
            brick_counts.astype(jnp.float32),
            jnp.zeros((PAD_ROWS * channels - 2 * k_width - 1,), jnp.float32),
        ]
    ).reshape(PAD_ROWS, channels)
    summed = sum_over_atoms(jnp.concatenate([factor, extra], axis=0))
    factor = summed[: 2 * k_width]
    extra = summed[2 * k_width :].reshape(-1)
    charge_sum = extra[: 2 * k_width]
    live_total = extra[2 * k_width]
    k_vectors, k_square = k_geometry(k_indices)
    kernel = teacher_kernel(k_square, smearing, inv_root)
    weighted = (jnp.concatenate([kernel, kernel], axis=0) * factor).astype(jnp.bfloat16)
    potential = jnp.dot(phases, weighted, preferred_element_type=jnp.float32)
    charged = (features.astype(jnp.float32) * teacher_charge[None, :]).astype(jnp.bfloat16)
    contracted = lax.dot_general(
        charged, weighted, (((1,), (1,)), ((), ())), preferred_element_type=jnp.float32
    )
    cosines = phases[:, :k_width].astype(jnp.float32)
    sines = phases[:, k_width:].astype(jnp.float32)
    force_terms = sines * contracted[:, :k_width] - cosines * contracted[:, k_width:]
    teacher_force = jnp.dot(force_terms, k_vectors.T, precision=HIGHEST_PRECISION)
    table = student_table(k_vectors, k_square, charge_sum, student_smear, inv_root, k_width)
    student_part = jnp.dot(phases, table, preferred_element_type=jnp.float32)
    packed = jnp.concatenate(
        [potential, teacher_force, student_part, jnp.zeros((atom_rows, 1), jnp.float32)], axis=1
    )
    own = lax.psum_scatter(packed, KA_AXES, scatter_dimension=0, tiled=True)
    share_rows = atom_rows // ka_groups
    ka_index = lax.axis_index(KA_AXES)
    row_start = ka_index * share_rows

    def own_rows(values):
        return lax.dynamic_slice_in_dim(values, row_start, share_rows, 0)

    teacher_features, teacher_out, forces, student_energy, misfit = finish(
        own[:, :channels],
        own[:, channels : channels + 3],
        own[:, channels + 3 : channels + 7],
        own_rows(features),
        own_rows(charge),
        own_rows(live_mask),
        norm_gain,
        w_mix,
        w_read,
    )
    loss_sum = functools.reduce(lambda v, axis: lax.psum(v, axis), ALL_AXES, jnp.sum(misfit))
    return (teacher_features, teacher_out.T, forces.T, student_energy, loss_sum / live_total)


def solution(mesh):
    sizes = dict(mesh.shape)
    ka = sizes["ka"]
    atom = sizes["atom"]
    cores = 2
    z_lo = ka // cores
    devices = mesh.devices.reshape(-1)
    y_size = 8 if atom % 8 == 0 else 1
    rest = atom // y_size
    zh = 2 if rest % 2 == 0 else 1
    x_size = rest // zh
    fine = Mesh(devices.reshape(y_size, x_size, zh, z_lo, cores), ALL_AXES)
    atom_spec = ATOM_AXES
    in_specs = (
        P(atom_spec, None),
        P(None, atom_spec),
        P(None, KA_AXES),
        P(atom_spec),
        P(atom_spec),
        P(),
        P(),
        P(),
        P(),
        P(),
        P(),
        P(),
        P(),
        P(),
        P(),
    )
    out_specs = (P(ALL_AXES, None), P(None, ALL_AXES), P(None, ALL_AXES), P(ALL_AXES), P())
    return jax.shard_map(local, mesh=fine, in_specs=in_specs, out_specs=out_specs, check_vma=False)
```

profile of v0, /device:TPU:1, one launch (start us, length us, event | category | flops | bytes accessed | tf_op | source)
XLA Modules:
  0.0 326.0 jit_solution(14616286438022679318)
XLA Ops:
  9.5 1.6 fusion.69
  11.2 1.4 fusion.14
  12.6 1.7 convolution_add_fusion
  16.2 17.6 %cosine_convert_fusion = (bf16[2048,512]{1,0:T(8,128)(2,1)S(1)}, bf16[2048,512]{1,0:T(8,128)(2,1)S(1)}) fusion(f32[512]{0:T(512)S(1)} %bitcast.109, f32[2048]{0:T(1024)S(1)} %bitcast.101, f32[512]{0:T(512)S(1)} %bitcast.111, f32[2048]{0:T(1024)S(1)} %bitcast.103, f32[512]{0:T(512)S(1)} %bitcast.107, f32[2048]{0:T(1024)S(1)} %bitcast.99), kind=kLoop, calls=%fused_computation.8 | loop fusion | flops 8388608 | bytes 4225024 | tf_op jit(solution)/shard_map/slice | solution.py:165
  35.8 3.0 concatenate.22
  39.9 3.2 fusion.15
  44.4 43.4 %reduce-scatter.4.cloned.1.call-done = f32[160,256]{1,0:T(8,128)} async-done(((f32[1280,256]{1,0:T(8,128)}), f32[160,256]{1,0:T(8,128)}) %reduce-scatter.4.cloned.1.call-update) | async-done | bytes 163856 | tf_op jit(solution)/shard_map/reduce_scatter | solution.py:100
  87.8 29.4 %reduce-scatter.6.cloned.1.call-done = f32[40,256]{1,0:T(8,128)} async-done(((f32[160,256]{1,0:T(8,128)}), f32[40,256]{1,0:T(8,128)}) %reduce-scatter.6.cloned.1.call-update) | async-done | bytes 40976 | tf_op jit(solution)/shard_map/reduce_scatter | solution.py:101
  117.2 16.1 %psum.42 = f32[40,256]{1,0:T(8,128)S(1)} all-reduce(f32[40,256]{1,0:T(8,128)} %reduce-scatter.6.cloned.1.call-done), channel_id=1, replica_groups=mesh['y'=8,'x'=4,'zh'=2,'zl'=4,'core'=2] {'zh'}, use_global_device_ids=true, to_apply=%region_2.3 | all-reduce | flops 10240 | bytes 81920 | tf_op jit(solution)/shard_map/psum | solution.py:102
  133.3 9.9 %all_gather.6 = f32[160,256]{1,0:T(8,128)} all-gather(f32[40,256]{1,0:T(8,128)S(1)} %psum.42), channel_id=1, replica_groups=mesh['y'=8,'x'=4,'zh'=2,'zl'=4,'core'=2] {'x'}, dimensions={0}, use_global_device_ids=true | all-gather | bytes 204800 | tf_op jit(solution)/shard_map/all_gather | solution.py:103
  145.9 36.9 %all-gather.2.cloned.1.call-done = f32[1280,256]{1,0:T(8,128)} async-done(((f32[160,256]{1,0:T(8,128)}), f32[1280,256]{1,0:T(8,128)}) %all-gather.2.cloned.1.call-update) | async-done | bytes 1310736 | tf_op jit(solution)/shard_map/all_gather | solution.py:104
  183.7 2.5 fusion.5
  186.3 20.6 %fusion.1 = f32[2048,3]{0,1:T(4,128)S(1)} fusion(f32[2048,1024]{1,0:T(8,128)S(1)} %fusion.5, s32[3,512]{1,0:T(4,128)S(1)} %copy-done.9, f32[512]{0:T(512)S(1)} %bitcast.110, f32[2048]{0:T(1024)S(1)} %bitcast.102, f32[512]{0:T(512)S(1)} %bitcast.112, f32[2048]{0:T(1024)S(1)} %bitcast.104, f32[512]{0:T(512)S(1)} %bitcast.108, f32[2048]{0:T(1024)S(1)} %bitcast.100), kind=kOutput, calls=%fused_computation.2 | convolution fusion | flops 51383296 | bytes 8450048 | tf_op jit(solution)/shard_map/dot_general | solution.py:168
  208.3 1.3 fusion.59
  209.7 1.6 maximum_maximum_fusion
  212.0 44.2 %reduce-scatter.8.cloned.1.call-done = f32[256,264]{0,1:T(8,128)} async-done(((f32[2048,264]{0,1:T(8,128)}), f32[256,264]{0,1:T(8,128)}) %reduce-scatter.8.cloned.1.call-update) | async-done | bytes 270352 | tf_op jit(solution)/shard_map/reduce_scatter | solution.py:174
  257.2 2.0 fusion.68
  260.2 1.4 multiply_reduce_fusion.1
  261.6 1.9 multiply_reduce_fusion.2
  263.5 13.9 %psum.43 = f32[]{:T(128)} all-reduce(f32[]{:T(128)} %get-tuple-element.5), channel_id=1, replica_groups=mesh['y'=8,'x'=4,'zh'=2,'zl'=4,'core'=2] {'y'}, use_global_device_ids=true, to_apply=%region_7.8 | all-reduce | flops 1 | bytes 8 | tf_op jit(solution)/shard_map/psum | solution.py:193
  277.4 9.0 %psum.44 = f32[]{:T(128)} all-reduce(f32[]{:T(128)} %psum.43), channel_id=1, replica_groups=mesh['y'=8,'x'=4,'zh'=2,'zl'=4,'core'=2] {'x'}, use_global_device_ids=true, to_apply=%region_8.9 | all-reduce | flops 1 | bytes 8 | tf_op jit(solution)/shard_map/psum | solution.py:193
  286.5 8.3 %psum.45 = f32[]{:T(128)} all-reduce(f32[]{:T(128)} %psum.44), channel_id=1, replica_groups=mesh['y'=8,'x'=4,'zh'=2,'zl'=4,'core'=2] {'zh'}, use_global_device_ids=true, to_apply=%region_9.10 | all-reduce | flops 1 | bytes 8 | tf_op jit(solution)/shard_map/psum | solution.py:193
  294.9 11.2 %psum.46 = f32[]{:T(128)} all-reduce(f32[]{:T(128)} %psum.45), channel_id=1, replica_groups=mesh['y'=8,'x'=4,'zh'=2,'zl'=4,'core'=2] {'zl'}, use_global_device_ids=true, to_apply=%region_10.11 | all-reduce | flops 1 | bytes 8 | tf_op jit(solution)/shard_map/psum | solution.py:193
  306.7 10.5 %psum.47 = f32[]{:T(128)} all-reduce(f32[]{:T(128)} %psum.46), channel_id=1, replica_groups=mesh['y'=8,'x'=4,'zh'=2,'zl'=4,'core'=2] {'core'}, use_global_device_ids=true, to_apply=%region_11.12 | all-reduce | flops 1 | bytes 8 | tf_op jit(solution)/shard_map/psum | solution.py:193
  (79 shorter events, 15.5 us)
Async XLA Ops:
  7.2 250.0 %copy-start = (bf16[256,256]{1,0:T(8,128)(2,1)S(1)}, bf16[256,256]{1,0:T(8,128)(2,1)}, u32[]{:S(2)}) copy-start(bf16[256,256]{1,0:T(8,128)(2,1)} %param.23) | copy-start | bytes 393220
  7.2 7.1 %copy-start.18 = (f32[128]{0:T(128)S(1)}, f32[128]{0:T(128)}, u32[]{:S(2)}) copy-start(f32[128]{0:T(128)} %param.27) | copy-start | bytes 1540
  7.2 80.6 %reduce-scatter.4.cloned.1.call-start = ((), (), s32[]{:S(2)}) async-start(), calls=%async_computation.3 | async-start | bytes 1474560 | tf_op jit(solution)/shard_map/reduce_scatter | solution.py:100
  8.1 8.0 %copy-start.7 = (f32[1,2048]{1,0:T(1,128)}, f32[1,2048]{1,0:T(1,128)S(1)}, u32[]{:S(2)}) copy-start(f32[1,2048]{1,0:T(1,128)S(1)} %get-tuple-element.23) | copy-start | bytes 24580
  8.9 7.3 %copy-start.10 = (f32[1,512]{1,0:T(1,128)}, f32[1,512]{1,0:T(1,128)S(1)}, u32[]{:S(2)}) copy-start(f32[1,512]{1,0:T(1,128)S(1)} %get-tuple-element.34) | copy-start | bytes 6148
  8.9 7.3 %copy-start.12 = (f32[1,512]{1,0:T(1,128)}, f32[1,512]{1,0:T(1,128)S(1)}, u32[]{:S(2)}) copy-start(f32[1,512]{1,0:T(1,128)S(1)} %get-tuple-element.35) | copy-start | bytes 6148
  8.9 7.3 %copy-start.14 = (f32[1,512]{1,0:T(1,128)}, f32[1,512]{1,0:T(1,128)S(1)}, u32[]{:S(2)}) copy-start(f32[1,512]{1,0:T(1,128)S(1)} %get-tuple-element.36) | copy-start | bytes 6148
  33.8 1.3 copy-start.4
  33.8 9.3 %copy-start.2 = (bf16[2048,512]{1,0:T(8,128)(2,1)}, bf16[2048,512]{1,0:T(8,128)(2,1)S(1)}, u32[]{:S(2)}) copy-start(bf16[2048,512]{1,0:T(8,128)(2,1)S(1)} %get-tuple-element.24) | copy-start | bytes 6291460
  33.8 6.1 %copy-start.1 = (bf16[2048,256]{1,0:T(8,128)(2,1)S(1)}, bf16[2048,256]{1,0:T(8,128)(2,1)}, u32[]{:S(2)}) copy-start(bf16[2048,256]{1,0:T(8,128)(2,1)} %param.15) | copy-start | bytes 3145732
  44.3 72.9 %reduce-scatter.6.cloned.1.call-start = ((), (), s32[]{:S(2)}) async-start(), calls=%async_computation.4 | async-start | bytes 204800 | tf_op jit(solution)/shard_map/reduce_scatter | solution.py:101
  87.8 95.0 %all-gather.2.cloned.1.call-start = ((), (), s32[]{:S(2)}) async-start(), calls=%async_computation.5 | async-start | bytes 1474560 | tf_op jit(solution)/shard_map/all_gather | solution.py:104
  143.2 113.0 %reduce-scatter.8.cloned.1.call-start = ((), (), s32[]{:S(2)}) async-start(), calls=%async_computation.6 | async-start | bytes 2433024 | tf_op jit(solution)/shard_map/reduce_scatter | solution.py:174
  183.6 2.6 copy-start.8
  183.6 2.6 copy-start.9
  183.6 2.6 copy-start.11
  183.6 2.6 copy-start.13
  183.6 2.6 copy-start.15
  186.3 20.7 %copy-start.3 = (bf16[2048,512]{1,0:T(8,128)(2,1)S(1)}, bf16[2048,512]{1,0:T(8,128)(2,1)}, u32[]{:S(2)}) copy-start(bf16[2048,512]{1,0:T(8,128)(2,1)} %copy-done.2) | copy-start | bytes 6291460
  186.3 20.7 %copy-start.5 = (bf16[2048,512]{1,0:T(8,128)(2,1)S(1)}, bf16[2048,512]{1,0:T(8,128)(2,1)}, u32[]{:S(2)}) copy-start(bf16[2048,512]{1,0:T(8,128)(2,1)} %copy-done.4) | copy-start | bytes 6291460
  207.0 1.3 copy-start.6
  209.6 47.6 %copy-start.17 = (f32[256]{0:T(256)S(1)}, f32[256]{0:T(256)}, u32[]{:S(2)}) copy-start(f32[256]{0:T(256)} %param.22) | copy-start | bytes 3076
  209.7 49.5 %copy-start.16 = (f32[256]{0:T(256)S(1)}, f32[256]{0:T(256)}, u32[]{:S(2)}) copy-start(f32[256]{0:T(256)} %param.24) | copy-start | bytes 3076
Sparse Core Ops, SparseCore 0:
  44.5 43.2 reduce-scatter.3
  90.6 26.6 reduce-scatter.5
  143.3 39.4 all-gather.1
  211.4 44.7 reduce-scatter.7
where the time goes:
time: 327 us; the launch traced here: 326 us
  waiting for transfers between devices  154 us (47%)
  blocking collectives  79 us (24%)
  matrix products  37.7 us (12%)
  other arithmetic  27.7 us (8%)
  between operations  17.9 us (5%)
  local copies, waits for them, and re-layouts  9.57 us (3%)
    psum x5, blocking collectives, local(): lax.psum(v, axis)  53 us
    reduce_scatter x1, waiting for transfers between devices, local(): own = lax.psum_scatter(packed, KA_AXES, scatter_dimension=0, tiled=True)  44.2 us
    reduce_scatter x1, waiting for transfers between devices, sum_over_atoms(): part = lax.psum_scatter(payload, 'y', scatter_dimension=0, tiled=True)  43.4 us
    all_gather x1, waiting for transfers between devices, sum_over_atoms(): return lax.all_gather(part, 'y', axis=0, tiled=True)  36.9 us
    reduce_scatter x1, waiting for transfers between devices, sum_over_atoms(): part = lax.psum_scatter(part, 'x', scatter_dimension=0, tiled=True)  29.4 us
    dot_general x1, matrix products, local(): jnp.dot(force_terms, k_vectors.T, precision=HIGHEST_PRECISION)  20.6 us
    slice x1, other arithmetic, local(): cosines = phases[:, :k_width].astype(jnp.float32)  17.6 us
    psum x1, blocking collectives, sum_over_atoms(): part = lax.psum(part, 'zh')  16.1 us
  transfers between devices with their start and end apart: 4, of which 4 were waited for; matrix products, arithmetic and copies ran while one was open for 1% of the time, Pallas kernels for 0%

commit v1 on v0

--- a/solution.py
+++ b/solution.py
@@ -101,7 +101,9 @@
     part = lax.psum_scatter(part, "x", scatter_dimension=0, tiled=True)
     part = lax.psum(part, "zh")
     part = lax.all_gather(part, "x", axis=0, tiled=True)
-    return lax.all_gather(part, "y", axis=0, tiled=True)
+    return jnp.concatenate(
+        lax.all_to_all(jnp.stack([part] * lax.axis_size("y")), "y", 0, 0), axis=0
+    )
 
 
 def local(

time: 327 us -> 316 us (0.966)
  waiting for transfers between devices: 154 us -> 137 us
  starting transfers between devices: 0.34 us -> 6.59 us
    all_gather x1 -> x0, waiting for transfers between devices: 36.9 us -> none  [sum_over_atoms(): return lax.all_gather(part, 'y', axis=0, tiled=True)]
    all_to_all x0 -> x1, waiting for transfers between devices: none -> 28.8 us  [sum_over_atoms(): lax.all_to_all(jnp.stack([part] * lax.axis_size('y')), 'y', 0, 0)]
    reduce_scatter x1, waiting for transfers between devices: 44.2 us -> 35.5 us  [local(): own = lax.psum_scatter(packed, KA_AXES, scatter_dimension=0, tiled=True)]
    all_to_all x0 -> x1, starting transfers between devices: none -> 6.48 us  [sum_over_atoms(): lax.all_to_all(jnp.stack([part] * lax.axis_size('y')), 'y', 0, 0)]
  transfers between devices with their start and end apart: 4 -> 4, of which waited for: 4 -> 4; matrix products, arithmetic and copies ran while one was open for 1% -> 0% of each run, Pallas kernels for 0% -> 0%
where the time goes in v1:
time: 316 us; the launch traced here: 315 us
  waiting for transfers between devices  137 us (43%)
  blocking collectives  78.6 us (25%)
  matrix products  38.7 us (12%)
  other arithmetic  26.3 us (8%)
  between operations  17.8 us (6%)
  local copies, waits for them, and re-layouts  9.85 us (3%)
  starting transfers between devices  6.59 us (2%)
    psum x5, blocking collectives, local(): lax.psum(v, axis)  53.1 us
    reduce_scatter x1, waiting for transfers between devices, sum_over_atoms(): part = lax.psum_scatter(payload, 'y', scatter_dimension=0, tiled=True)  43.4 us
    reduce_scatter x1, waiting for transfers between devices, local(): own = lax.psum_scatter(packed, KA_AXES, scatter_dimension=0, tiled=True)  35.5 us
    reduce_scatter x1, waiting for transfers between devices, sum_over_atoms(): part = lax.psum_scatter(part, 'x', scatter_dimension=0, tiled=True)  29.4 us
    all_to_all x1, waiting for transfers between devices, sum_over_atoms(): lax.all_to_all(jnp.stack([part] * lax.axis_size('y')), 'y', 0, 0)  28.8 us
    dot_general x1, matrix products, local(): jnp.dot(force_terms, k_vectors.T, precision=HIGHEST_PRECISION)  20.6 us
    slice x1, other arithmetic, local(): cosines = phases[:, :k_width].astype(jnp.float32)  17.6 us
    psum x1, blocking collectives, sum_over_atoms(): part = lax.psum(part, 'zh')  16.1 us
  transfers between devices with their start and end apart: 4, of which 4 were waited for; matrix products, arithmetic and copies ran while one was open for 0% of the time, Pallas kernels for 0%

profile of v1, /device:TPU:1, one launch (start us, length us, event | category | flops | bytes accessed | tf_op | source)
XLA Modules:
  0.0 315.0 jit_solution(17429110864755591134)
XLA Ops:
  9.5 1.6 fusion.69
  11.2 1.4 fusion.14
  12.6 1.7 convolution_add_fusion
  16.2 17.6 %cosine_convert_fusion = (bf16[2048,512]{1,0:T(8,128)(2,1)S(1)}, bf16[2048,512]{1,0:T(8,128)(2,1)S(1)}) fusion(f32[512]{0:T(512)S(1)} %bitcast.114, f32[2048]{0:T(1024)S(1)} %bitcast.106, f32[512]{0:T(512)S(1)} %bitcast.116, f32[2048]{0:T(1024)S(1)} %bitcast.108, f32[512]{0:T(512)S(1)} %bitcast.112, f32[2048]{0:T(1024)S(1)} %bitcast.104), kind=kLoop, calls=%fused_computation.8 | loop fusion | flops 8388608 | bytes 4225024 | tf_op jit(solution)/shard_map/slice | solution.py:167
  35.8 3.0 concatenate.22
  39.9 3.2 %fusion.15 = f32[1024,256]{1,0:T(8,128)S(1)} fusion(bf16[2048,256]{1,0:T(8,128)(2,1)S(1)} %copy-done.1, bf16[2048]{0:T(1024)(128)(2,1)S(1)} %fusion.41, bf16[2048,512]{1,0:T(8,128)(2,1)} %copy-done.4, bf16[2048,512]{1,0:T(8,128)(2,1)S(1)} %get-tuple-element.24), kind=kOutput, calls=%fused_computation.26 | convolution fusion | flops 1082654720 | bytes 6295552 | tf_op jit(solution)/shard_map/dot_general | solution.py:143
  44.4 43.4 %reduce-scatter.4.cloned.1.call-done = f32[160,256]{1,0:T(8,128)} async-done(((f32[1280,256]{1,0:T(8,128)}), f32[160,256]{1,0:T(8,128)}) %reduce-scatter.4.cloned.1.call-update) | async-done | bytes 163856 | tf_op jit(solution)/shard_map/reduce_scatter | solution.py:100
  87.8 29.4 %reduce-scatter.6.cloned.1.call-done = f32[40,256]{1,0:T(8,128)} async-done(((f32[160,256]{1,0:T(8,128)}), f32[40,256]{1,0:T(8,128)}) %reduce-scatter.6.cloned.1.call-update) | async-done | bytes 40976 | tf_op jit(solution)/shard_map/reduce_scatter | solution.py:101
  117.2 16.1 %psum.42 = f32[40,256]{1,0:T(8,128)S(1)} all-reduce(f32[40,256]{1,0:T(8,128)} %reduce-scatter.6.cloned.1.call-done), channel_id=1, replica_groups=mesh['y'=8,'x'=4,'zh'=2,'zl'=4,'core'=2] {'zh'}, use_global_device_ids=true, to_apply=%region_2.3 | all-reduce | flops 10240 | bytes 81920 | tf_op jit(solution)/shard_map/psum | solution.py:102
  133.3 9.5 %all_gather.3 = f32[160,256]{1,0:T(8,128)S(1)} all-gather(f32[40,256]{1,0:T(8,128)S(1)} %psum.42), channel_id=1, replica_groups=mesh['y'=8,'x'=4,'zh'=2,'zl'=4,'core'=2] {'x'}, dimensions={0}, use_global_device_ids=true | all-gather | bytes 204800 | tf_op jit(solution)/shard_map/all_gather | solution.py:103
  143.9 6.5 %all-to-all-start = ((f32[8,160,256]{2,1,0:T(8,128)}), f32[8,160,256]{2,1,0:T(8,128)S(1)}, u32[]{:S(2)}, u32[]{:S(2)}) async-start(f32[8,160,256]{2,1,0:T(8,128)} %stack.8), calls=%async_computation.2 | async-start | bytes 2621440 | tf_op jit(solution)/shard_map/all_to_all | solution.py:105
  151.5 28.8 %all-to-all-done = f32[8,160,256]{2,1,0:T(8,128)S(1)} async-done(((f32[8,160,256]{2,1,0:T(8,128)}), f32[8,160,256]{2,1,0:T(8,128)S(1)}, u32[]{:S(2)}, u32[]{:S(2)}) %all-to-all-start) | async-done | bytes 1310752 | tf_op jit(solution)/shard_map/all_to_all | solution.py:105
  180.3 3.5 %fusion.59 = f32[2048,256]{0,1:T(8,128)S(1)} fusion(bf16[2048,512]{1,0:T(8,128)(2,1)} %copy-done.4, bf16[2048,512]{1,0:T(8,128)(2,1)} %copy-done.2, f32[1280,256]{1,0:T(8,128)S(1)} %bitcast.100, f32[512,256]{1,0:T(8,128)S(1)} %divide_multiply_fusion), kind=kOutput, calls=%fused_computation.99 | convolution fusion | flops 1082916864 | bytes 7864320 | tf_op jit(solution)/shard_map/dot_general | solution.py:162
  185.2 20.6 %fusion.1 = f32[2048,3]{0,1:T(4,128)S(1)} fusion(f32[2048,1024]{1,0:T(8,128)S(1)} %fusion.5, s32[3,512]{1,0:T(4,128)S(1)} %copy-done.8, f32[512]{0:T(512)S(1)} %bitcast.115, f32[2048]{0:T(1024)S(1)} %bitcast.107, f32[512]{0:T(512)S(1)} %bitcast.117, f32[2048]{0:T(1024)S(1)} %bitcast.109, f32[512]{0:T(512)S(1)} %bitcast.113, f32[2048]{0:T(1024)S(1)} %bitcast.105), kind=kOutput, calls=%fused_computation.2 | convolution fusion | flops 51383296 | bytes 8450048 | tf_op jit(solution)/shard_map/dot_general | solution.py:170
  207.1 1.6 maximum_maximum_fusion
  209.5 35.5 %reduce-scatter.8.cloned.1.call-done = f32[256,264]{0,1:T(8,128)} async-done(((f32[2048,264]{0,1:T(8,128)}), f32[256,264]{0,1:T(8,128)}) %reduce-scatter.8.cloned.1.call-update) | async-done | bytes 270352 | tf_op jit(solution)/shard_map/reduce_scatter | solution.py:176
  246.0 2.0 fusion.68
  249.0 1.4 multiply_reduce_fusion.1
  250.4 1.9 multiply_reduce_fusion.2
  252.3 14.0 %psum.43 = f32[]{:T(128)} all-reduce(f32[]{:T(128)} %get-tuple-element.5), channel_id=1, replica_groups=mesh['y'=8,'x'=4,'zh'=2,'zl'=4,'core'=2] {'y'}, use_global_device_ids=true, to_apply=%region_7.8 | all-reduce | flops 1 | bytes 8 | tf_op jit(solution)/shard_map/psum | solution.py:195
  266.3 8.7 %psum.44 = f32[]{:T(128)} all-reduce(f32[]{:T(128)} %psum.43), channel_id=1, replica_groups=mesh['y'=8,'x'=4,'zh'=2,'zl'=4,'core'=2] {'x'}, use_global_device_ids=true, to_apply=%region_8.9 | all-reduce | flops 1 | bytes 8 | tf_op jit(solution)/shard_map/psum | solution.py:195
  275.0 8.3 %psum.45 = f32[]{:T(128)} all-reduce(f32[]{:T(128)} %psum.44), channel_id=1, replica_groups=mesh['y'=8,'x'=4,'zh'=2,'zl'=4,'core'=2] {'zh'}, use_global_device_ids=true, to_apply=%region_9.10 | all-reduce | flops 1 | bytes 8 | tf_op jit(solution)/shard_map/psum | solution.py:195
  283.5 11.5 %psum.46 = f32[]{:T(128)} all-reduce(f32[]{:T(128)} %psum.45), channel_id=1, replica_groups=mesh['y'=8,'x'=4,'zh'=2,'zl'=4,'core'=2] {'zl'}, use_global_device_ids=true, to_apply=%region_10.11 | all-reduce | flops 1 | bytes 8 | tf_op jit(solution)/shard_map/psum | solution.py:195
  295.4 10.6 %psum.47 = f32[]{:T(128)} all-reduce(f32[]{:T(128)} %psum.46), channel_id=1, replica_groups=mesh['y'=8,'x'=4,'zh'=2,'zl'=4,'core'=2] {'core'}, use_global_device_ids=true, to_apply=%region_11.12 | all-reduce | flops 1 | bytes 8 | tf_op jit(solution)/shard_map/psum | solution.py:195
  (81 shorter events, 15.3 us)
Async XLA Ops:
  7.2 238.8 %copy-start = (bf16[256,256]{1,0:T(8,128)(2,1)S(1)}, bf16[256,256]{1,0:T(8,128)(2,1)}, u32[]{:S(2)}) copy-start(bf16[256,256]{1,0:T(8,128)(2,1)} %param.23) | copy-start | bytes 393220
  7.2 7.1 %copy-start.19 = (f32[128]{0:T(128)S(1)}, f32[128]{0:T(128)}, u32[]{:S(2)}) copy-start(f32[128]{0:T(128)} %param.27) | copy-start | bytes 1540
  7.2 80.6 %reduce-scatter.4.cloned.1.call-start = ((), (), s32[]{:S(2)}) async-start(), calls=%async_computation.4 | async-start | bytes 1474560 | tf_op jit(solution)/shard_map/reduce_scatter | solution.py:100
  8.1 8.0 %copy-start.6 = (f32[1,2048]{1,0:T(1,128)}, f32[1,2048]{1,0:T(1,128)S(1)}, u32[]{:S(2)}) copy-start(f32[1,2048]{1,0:T(1,128)S(1)} %get-tuple-element.23) | copy-start | bytes 24580
  8.9 7.3 %copy-start.9 = (f32[1,512]{1,0:T(1,128)}, f32[1,512]{1,0:T(1,128)S(1)}, u32[]{:S(2)}) copy-start(f32[1,512]{1,0:T(1,128)S(1)} %get-tuple-element.34) | copy-start | bytes 6148
  8.9 7.3 %copy-start.11 = (f32[1,512]{1,0:T(1,128)}, f32[1,512]{1,0:T(1,128)S(1)}, u32[]{:S(2)}) copy-start(f32[1,512]{1,0:T(1,128)S(1)} %get-tuple-element.35) | copy-start | bytes 6148
  8.9 7.3 %copy-start.13 = (f32[1,512]{1,0:T(1,128)}, f32[1,512]{1,0:T(1,128)S(1)}, u32[]{:S(2)}) copy-start(f32[1,512]{1,0:T(1,128)S(1)} %get-tuple-element.36) | copy-start | bytes 6148
  33.8 1.3 copy-start.4
  33.8 9.3 %copy-start.2 = (bf16[2048,512]{1,0:T(8,128)(2,1)}, bf16[2048,512]{1,0:T(8,128)(2,1)S(1)}, u32[]{:S(2)}) copy-start(bf16[2048,512]{1,0:T(8,128)(2,1)S(1)} %get-tuple-element.24) | copy-start | bytes 6291460
  33.8 6.1 %copy-start.1 = (bf16[2048,256]{1,0:T(8,128)(2,1)S(1)}, bf16[2048,256]{1,0:T(8,128)(2,1)}, u32[]{:S(2)}) copy-start(bf16[2048,256]{1,0:T(8,128)(2,1)} %param.15) | copy-start | bytes 3145732
  44.3 106.8 %copy-start.15 = (f32[256]{0:T(256)S(1)}, f32[256]{0:T(256)}, u32[]{:S(2)}) copy-start(f32[256]{0:T(256)} %param.20) | copy-start | bytes 3076
  44.3 106.9 %copy-start.8 = (s32[3,512]{1,0:T(4,128)S(1)}, s32[3,512]{1,0:T(4,128)}, u32[]{:S(2)}) copy-start(s32[3,512]{1,0:T(4,128)} %param.17) | copy-start | bytes 18436
  44.3 72.9 %reduce-scatter.6.cloned.1.call-start = ((), (), s32[]{:S(2)}) async-start(), calls=%async_computation.5 | async-start | bytes 204800 | tf_op jit(solution)/shard_map/reduce_scatter | solution.py:101
  143.9 36.3 %all-to-all-start = ((f32[8,160,256]{2,1,0:T(8,128)}), f32[8,160,256]{2,1,0:T(8,128)S(1)}, u32[]{:S(2)}, u32[]{:S(2)}) async-start(f32[8,160,256]{2,1,0:T(8,128)} %stack.8), calls=%async_computation.2 | async-start | bytes 2621440 | tf_op jit(solution)/shard_map/all_to_all | solution.py:105
  150.4 94.6 %reduce-scatter.8.cloned.1.call-start = ((), (), s32[]{:S(2)}) async-start(), calls=%async_computation.6 | async-start | bytes 2433024 | tf_op jit(solution)/shard_map/reduce_scatter | solution.py:176
  180.3 3.5 %copy-start.16 = (f32[256]{0:T(256)S(1)}, f32[256]{0:T(256)}, u32[]{:S(2)}) copy-start(f32[256]{0:T(256)} %param.21) | copy-start | bytes 3076
  183.8 1.3 copy-start.7
  183.8 1.3 copy-start.10
  183.8 1.3 copy-start.12
  183.9 1.3 copy-start.14
  185.2 20.7 %copy-start.3 = (bf16[2048,512]{1,0:T(8,128)(2,1)S(1)}, bf16[2048,512]{1,0:T(8,128)(2,1)}, u32[]{:S(2)}) copy-start(bf16[2048,512]{1,0:T(8,128)(2,1)} %copy-done.2) | copy-start | bytes 6291460
  185.2 20.7 %copy-start.5 = (bf16[2048,512]{1,0:T(8,128)(2,1)S(1)}, bf16[2048,512]{1,0:T(8,128)(2,1)}, u32[]{:S(2)}) copy-start(bf16[2048,512]{1,0:T(8,128)(2,1)} %copy-done.4) | copy-start | bytes 6291460
  207.1 38.9 %copy-start.18 = (f32[256]{0:T(256)S(1)}, f32[256]{0:T(256)}, u32[]{:S(2)}) copy-start(f32[256]{0:T(256)} %param.22) | copy-start | bytes 3076
  207.1 40.9 %copy-start.17 = (f32[256]{0:T(256)S(1)}, f32[256]{0:T(256)}, u32[]{:S(2)}) copy-start(f32[256]{0:T(256)} %param.24) | copy-start | bytes 3076
Sparse Core Ops, SparseCore 0:
  44.5 43.2 reduce-scatter.3
  90.6 26.6 reduce-scatter.5
  208.9 36.0 reduce-scatter.7
